TPU v7x, 256 devices: a whole 4x4x8 slice. The times are simulated.
256 devices in a mesh: req: 16 (over z, core), head: 16 (over x, y).
Axes of the slice: x: 4, y: 4, z: 8, core: 2. Of those that a mesh axis runs over, the one named last changes fastest.
Arguments:
- tree_heads: bfloat16 [4096, 16384], P(('req', 'head')), may hold values from -6 to 6
- tree_gates: bfloat16 [4096, 16384], P(('req', 'head')), may hold values from -6 to 6
- tree_steps: bfloat16 [4096, 256], P(('req', 'head')), may hold values from -6 to 6
- tree_groups: bfloat16 [4096, 4096], P(('req', 'head')), may hold values from -6 to 6
- new_tree: int32 [128, 32, 32], P('req'), may hold values from 0 to 1, as said below
- kernel_heads: bfloat16 [4, 16384], P(None, 'head'), may hold values from -3 to 3
- shift_heads: float32 [16384], P('head'), may hold values from -3 to 3
- kernel_groups: bfloat16 [4, 4096], replicated, may hold values from -3 to 3
- shift_groups: float32 [4096], replicated, may hold values from -3 to 3
- log_rates: float32 [256], P('head'), may hold values from 0 to 2.77
- step_bias: float32 [256], P('head'), may hold values from -6 to -2
- skip_gain: float32 [256], P('head'), may hold values from 0.5 to 1.5
- norm_gain: float32 [16384], P('head'), may hold values from 0.5 to 1.5
- old_state: bfloat16 [128, 256, 64, 256], P('req', 'head'), may hold values from -0.59765625 to 0.59765625
- old_heads: bfloat16 [128, 32, 16384], P('req', None, 'head'), may hold values from -3 to 3
- old_keys: bfloat16 [128, 32, 2048], P('req'), may hold values from -3 to 3
- old_steps: float32 [128, 32, 256], P('req', None, 'head'), may hold values from 0.002 to 0.2
- prior_heads: bfloat16 [128, 32, 16384], P('req', None, 'head'), may hold values from -6 to 6
- prior_groups: bfloat16 [128, 32, 4096], P('req', 'head'), may hold values from -6 to 6
- old_tree: int32 [128, 32, 32], P('req'), may hold values from 0 to 1, as said below
- accepted: int32 [128], P('req'), may hold values from 2 to 31, as said below
- new_owner: int32 [128], replicated, may hold values from 0 to 127, as said below
Outputs:
- mixed: bfloat16 [4096, 16384], P('req', 'head')
Inputs may be any that keep to these rules, and one draw needn't show every extreme that they name: `old_tree`: entry (t, j) is 1 when node j is node t or one of its ancestors, else 0; node 0 is the root, every parent has a lower number than its child, node 1 is the child of node 0 and node 2 the child of node 1, and every node numbered 2 or more has depth two or more. `new_tree`: ancestor masks of the same kind as old_tree. The accepted node has depth two or more in old_tree. A permutation of the slots. Slot i lives on device i // 8 of req before and on device new_owner[i] // 8 after; no old device hands more than 2 requests to one new device, and in every draw some pairs of devices carry exactly 2.
All inputs are finite; a program needn't handle non-finite values.
Results may differ from a plain program's by a relative error of at most 0.0052.
Values may be sent and summed in bfloat16 or wider, within the bound.
No kernel may reach another device: no remote copies, remote signals or barrier semaphores. Data moves between devices by JAX's collectives and lax.ppermute only.
A program may use at most 128 MiB of HBM per device.

v0:
```python
import jax
import jax.numpy as jnp
from jax import lax
from jax.sharding import PartitionSpec as P

HEADS = 256
HEAD_DIM = 64
STATE = 256
GROUPS = 8
NODES = 32
MOST = 2
EPSILON = 1e-05


def tree_conv(tree_rows, tail_rows, ancestry, weight, offset_bias):
    node_depth = jnp.sum(ancestry, axis=-1) - 1
    places = jnp.arange(3, dtype=jnp.int32)
    summed = weight[3].astype(jnp.float32) * tree_rows.astype(jnp.float32) + offset_bias
    for upward in range(1, 4):
        picked = (
            (ancestry == 1) & (node_depth[:, None, :] == node_depth[:, :, None] - upward)
        ).astype(jnp.bfloat16)
        older_rows = (places[None, None, :] == node_depth[:, :, None] - upward + 3).astype(
            jnp.bfloat16
        )
        shifted = jnp.einsum("btj,bjc->btc", picked, tree_rows, preferred_element_type=jnp.float32)
        shifted = shifted + jnp.einsum(
            "bti,bic->btc", older_rows, tail_rows, preferred_element_type=jnp.float32
        )
        summed = summed + weight[3 - upward].astype(jnp.float32) * shifted
    return jax.nn.silu(summed).astype(jnp.bfloat16)


def place_slots(payload, positions, count):
    wanted = jnp.arange(count, dtype=jnp.int32)
    owners = jnp.arange(positions.shape[0], dtype=jnp.int32)
    hits = positions[None, :] == wanted[:, None]
    chosen = jnp.sum(jnp.where(hits, owners[None, :], 0), axis=1)
    filled = jnp.any(hits, axis=1).reshape((count,) + (1,) * (payload.ndim - 1))
    taken = jnp.take(payload, chosen, axis=0)
    return jnp.where(filled, taken, jnp.zeros_like(taken))


def shards(
    tree_heads,
    tree_gates,
    tree_steps,
    tree_groups,
    new_tree,
    kernel_heads,
    shift_heads,
    kernel_groups,
    shift_groups,
    log_rates,
    step_bias,
    skip_gain,
    norm_gain,
    old_state,
    old_heads,
    old_keys,
    old_steps,
    prior_heads,
    prior_groups,
    old_tree,
    accepted,
    new_owner,
):
    req_count = lax.axis_size("req")
    req_index = lax.axis_index("req")
    head_index = lax.axis_index("head")
    reqs_dev = new_tree.shape[0]
    local_heads = log_rates.shape[0]
    local_nodes = prior_groups.shape[1]
    per_group = HEADS // GROUPS
    span_heads = min(local_heads, per_group)
    span_groups = local_heads // span_heads
    first_group = head_index * local_heads // per_group
    slot_count = req_count * MOST
    key_width = GROUPS * STATE
    highest = lax.Precision.HIGHEST
    owner_table = new_owner.reshape(req_count, reqs_dev)
    target_dev = owner_table // reqs_dev
    local_ids = jnp.arange(reqs_dev, dtype=jnp.int32)
    before = local_ids[None, :, None] > local_ids[None, None, :]
    same_dest = target_dev[:, :, None] == target_dev[:, None, :]
    arrival = jnp.sum((same_dest & before).astype(jnp.int32), axis=-1)
    send_table = target_dev * MOST + arrival
    send_pos = lax.dynamic_index_in_dim(send_table, req_index, 0, keepdims=False)
    wanted_slot = req_index * reqs_dev + local_ids
    all_ids = jnp.arange(new_owner.shape[0], dtype=jnp.int32)
    match = new_owner[None, :] == wanted_slot[:, None]
    anchor = jnp.sum(jnp.where(match, all_ids[None, :], 0), axis=1)
    recv_pos = anchor // reqs_dev * MOST + jnp.take(arrival.reshape(-1), anchor)
    decay_rates = -jnp.exp(log_rates)
    node_ids = jnp.arange(NODES, dtype=jnp.int32)
    chosen_hot = node_ids[None, :] == accepted[:, None]
    chosen_row = jnp.sum(jnp.where(chosen_hot[:, :, None], old_tree, 0), axis=1)
    old_depth = jnp.sum(old_tree, axis=-1) - 1
    chosen_depth = jnp.sum(jnp.where(chosen_hot, old_depth, 0), axis=1)
    places = jnp.arange(3, dtype=jnp.int32)
    lineage = chosen_row == 1
    tail_pick = (
        lineage[:, None, :]
        & (old_depth[:, None, :] == chosen_depth[:, None, None] - 2 + places[None, :, None])
    ).astype(jnp.bfloat16)
    tail_heads = jnp.einsum(
        "bij,bjc->bic", tail_pick, prior_heads, preferred_element_type=jnp.float32
    ).astype(jnp.bfloat16)
    pick_local = lax.dynamic_slice_in_dim(tail_pick, head_index * local_nodes, local_nodes, 2)
    tail_part = jnp.einsum(
        "bij,bjc->bic", pick_local, prior_groups, preferred_element_type=jnp.float32
    )
    tail_groups = lax.psum(tail_part.astype(jnp.bfloat16), "head")
    old_sums = jnp.einsum(
        "btj,bjh->bth", old_tree.astype(jnp.float32), old_steps * decay_rates, precision=highest
    )
    chosen_sum = jnp.sum(jnp.where(chosen_hot[:, :, None], old_sums, 0.0), axis=1)
    kept_weight = (
        jnp.where(
            lineage[:, :, None],
            jnp.exp(jnp.where(lineage[:, :, None], chosen_sum[:, None, :] - old_sums, 0.0)),
            0.0,
        )
        * old_steps
    )
    weighted = (
        (
            kept_weight[..., None]
            * old_heads.reshape(reqs_dev, NODES, local_heads, HEAD_DIM).astype(jnp.float32)
        )
        .astype(jnp.bfloat16)
        .reshape(reqs_dev, NODES, span_groups, span_heads, HEAD_DIM)
    )
    key_slice = lax.dynamic_slice_in_dim(
        old_keys, first_group * STATE, span_groups * STATE, 2
    ).reshape(reqs_dev, NODES, span_groups, STATE)
    update = jnp.einsum(
        "bjgqp,bjgn->bgqpn", weighted, key_slice, preferred_element_type=jnp.float32
    )
    carry_state = (
        jnp.exp(chosen_sum).reshape(reqs_dev, span_groups, span_heads, 1, 1)
        * old_state.reshape(reqs_dev, span_groups, span_heads, HEAD_DIM, STATE).astype(jnp.float32)
        + update
    ).astype(jnp.bfloat16)
    head_rows, gate_rows, step_rows = (
        lax.all_to_all(tree_heads, "head", split_axis=1, concat_axis=0, tiled=True),
        lax.all_to_all(tree_gates, "head", split_axis=1, concat_axis=0, tiled=True),
        lax.all_to_all(tree_steps, "head", split_axis=1, concat_axis=0, tiled=True),
    )
    group_rows = lax.all_gather(tree_groups, "head", axis=0, tiled=True)
    head_rows = head_rows.reshape(reqs_dev, NODES, -1)
    gate_rows = gate_rows.reshape(reqs_dev, NODES, span_groups, span_heads, HEAD_DIM)
    step_rows = step_rows.reshape(reqs_dev, NODES, local_heads)
    group_rows = group_rows.reshape(reqs_dev, NODES, -1)
    moved = (
        lax.all_to_all(
            place_slots(carry_state, send_pos, slot_count),
            "req",
            split_axis=0,
            concat_axis=0,
            tiled=True,
        ),
        lax.all_to_all(
            place_slots(tail_heads, send_pos, slot_count),
            "req",
            split_axis=0,
            concat_axis=0,
            tiled=True,
        ),
        lax.all_to_all(
            place_slots(tail_groups, send_pos, slot_count),
            "req",
            split_axis=0,
            concat_axis=0,
            tiled=True,
        ),
    )
    held_state = jnp.take(moved[0], recv_pos, axis=0)
    conv_heads = tree_conv(
        head_rows, jnp.take(moved[1], recv_pos, axis=0), new_tree, kernel_heads, shift_heads
    )
    conv_groups = tree_conv(
        group_rows, jnp.take(moved[2], recv_pos, axis=0), new_tree, kernel_groups, shift_groups
    )
    own_keys = lax.dynamic_slice_in_dim(conv_groups, first_group * STATE, span_groups * STATE, 2)
    own_queries = lax.dynamic_slice_in_dim(
        conv_groups, key_width + first_group * STATE, span_groups * STATE, 2
    )
    conv_heads, own_keys, own_queries = (conv_heads, own_keys, own_queries)
    query_four = own_queries.reshape(reqs_dev, NODES, span_groups, STATE)
    carried = jnp.einsum(
        "btgn,bgqpn->btgqp", query_four, held_state, preferred_element_type=jnp.float32
    )
    key_four = own_keys.reshape(reqs_dev, NODES, span_groups, STATE)
    step_sizes = jax.nn.softplus(step_rows.astype(jnp.float32) + step_bias)
    decay_sum = jnp.einsum(
        "btj,bjh->bth", new_tree.astype(jnp.float32), step_sizes * decay_rates, precision=highest
    )
    intersection = jnp.einsum(
        "btgn,bjgn->btjg", query_four, key_four, preferred_element_type=jnp.float32
    )
    lineage_new = (new_tree == 1)[:, :, :, None]
    decay_gap = decay_sum[:, :, None, :] - decay_sum[:, None, :, :]
    decays = jnp.where(lineage_new, jnp.exp(jnp.where(lineage_new, decay_gap, 0.0)), 0.0)
    mixing = (
        decays.reshape(reqs_dev, NODES, NODES, span_groups, span_heads)
        * intersection[..., None]
        * step_sizes.reshape(reqs_dev, 1, NODES, span_groups, span_heads)
    ).astype(jnp.bfloat16)
    values = conv_heads.reshape(reqs_dev, NODES, span_groups, span_heads, HEAD_DIM)
    inner_part = jnp.einsum(
        "btjgq,bjgqp->btgqp", mixing, values, preferred_element_type=jnp.float32
    )
    output = (
        inner_part
        + jnp.exp(decay_sum).reshape(reqs_dev, NODES, span_groups, span_heads, 1) * carried
        + skip_gain.reshape(1, 1, span_groups, span_heads, 1) * values.astype(jnp.float32)
    )
    gated_out = output * jax.nn.silu(gate_rows.astype(jnp.float32))
    group_power = jnp.sum(gated_out * gated_out, axis=(3, 4))
    zero_index = jnp.zeros((), jnp.int32)
    power_full = lax.dynamic_update_slice(
        jnp.zeros((reqs_dev, NODES, GROUPS), jnp.float32),
        group_power,
        (zero_index, zero_index, first_group),
    )
    power_total = lax.psum(power_full, "head")
    power_own = lax.dynamic_slice_in_dim(power_total, first_group, span_groups, 2)
    scale_factor = lax.rsqrt(power_own / (per_group * HEAD_DIM) + EPSILON)
    normed = (
        gated_out
        * scale_factor[..., None, None]
        * norm_gain.reshape(1, 1, span_groups, span_heads, HEAD_DIM)
    )
    return normed.reshape(reqs_dev * NODES, local_heads * HEAD_DIM).astype(jnp.bfloat16)


def solution(mesh):
    placed = (
        P(("req", "head"), None),
        P(("req", "head"), None),
        P(("req", "head"), None),
        P(("req", "head"), None),
        P("req", None, None),
        P(None, "head"),
        P("head"),
        P(),
        P(),
        P("head"),
        P("head"),
        P("head"),
        P("head"),
        P("req", "head", None, None),
        P("req", None, "head"),
        P("req", None, None),
        P("req", None, "head"),
        P("req", None, "head"),
        P("req", "head", None),
        P("req", None, None),
        P("req"),
        P(),
    )
    return jax.shard_map(
        shards, mesh=mesh, in_specs=placed, out_specs=P("req", "head"), check_vma=False
    )
```

profile of v0, /device:TPU:32, one launch (start us, length us, event | category | flops | bytes accessed | tf_op | source)
XLA Modules:
  0.0 639.1 jit_solution(553130558290788781)
XLA Ops:
  6.5 0.9 copy.90
  8.2 7.0 %all-to-all-start.2 = ((bf16[16,2,128]{2,1,0:T(2,128)(2,1)}), bf16[16,2,128]{2,1,0:T(2,128)(2,1)S(1)}, u32[]{:S(2)}, u32[]{:S(2)}) async-start(bf16[16,2,128]{2,1,0:T(2,128)(2,1)} %reshape.611), calls=%async_computation.2 | async-start | bytes 16384 | tf_op jit(solution)/shard_map/all_to_all | solution.py:148
  16.0 1.2 fusion.81
  18.2 2.0 convolution_convert_fusion
  21.6 1.4 convolution_convert_fusion.1
  23.8 1.0 select_select_fusion.1
  24.8 1.2 exponential_negate_fusion
  26.0 1.6 reshape.543
  27.7 1.9 copy.134
  29.6 1.9 copy.133
  31.5 8.6 %all-to-all-start.1 = ((bf16[32,3,1024]{2,1,0:T(4,128)(2,1)}), bf16[32,3,1024]{2,1,0:T(4,128)(2,1)}, u32[]{:S(2)}, u32[]{:S(2)}) async-start(bf16[32,3,1024]{2,1,0:T(4,128)(2,1)} %select_select_fusion.1), calls=%async_computation.1 | async-start | bytes 524288 | tf_op jit(solution)/shard_map/all_to_all | solution.py:163
  41.1 1.0 select_reduce_fusion.1
  42.3 7.5 %all-to-all-done.1 = bf16[32,3,1024]{2,1,0:T(4,128)(2,1)} async-done(((bf16[32,3,1024]{2,1,0:T(4,128)(2,1)}), bf16[32,3,1024]{2,1,0:T(4,128)(2,1)}, u32[]{:S(2)}, u32[]{:S(2)}) %all-to-all-start.1) | async-done | bytes 196640 | tf_op jit(solution)/shard_map/all_to_all | solution.py:163
  49.7 7.3 %all-to-all-start = ((bf16[16,16,1024]{2,0,1:T(8,128)(2,1)}), bf16[16,16,1024]{2,0,1:T(8,128)(2,1)}, u32[]{:S(2)}, u32[]{:S(2)}) async-start(bf16[16,16,1024]{2,0,1:T(8,128)(2,1)} %bitcast.122), calls=%async_computation | async-start | bytes 1048576 | tf_op jit(solution)/shard_map/all_to_all | solution.py:146
  57.0 5.6 add_convert_fusion
  62.7 9.3 %gather_fusion.5 = bf16[32,16,64,256]{3,2,1,0:T(8,128)(2,1)} fusion(bf16[8,16,64,256]{3,2,1,0:T(8,128)(2,1)} %add_convert_fusion, s32[1024]{0:T(1024)S(1)} %pad_clamp_fusion.1), kind=kCustom, calls=%fused_computation.5 | custom fusion | bytes 33554560 | tf_op jit(solution)/shard_map/jit(_take)/gather | solution.py:40
  72.0 47.8 %all-reduce.2.cloned.1.call-done = bf16[8,3,4096]{2,1,0:T(4,128)(2,1)} async-done(((bf16[8,3,4096]{2,1,0:T(4,128)(2,1)}), bf16[8,3,4096]{2,1,0:T(4,128)(2,1)}) %all-reduce.2.cloned.1.call-update) | async-done | bytes 196624 | tf_op jit(solution)/shard_map/psum | solution.py:113
  119.7 2.4 gather_fusion.3
  122.1 5.0 all-to-all-start.5
  127.2 1.7 select_select_fusion
  128.9 8.4 %all-to-all-done.5 = bf16[16,16,1024]{2,0,1:T(8,128)(2,1)S(1)} async-done(((bf16[16,16,1024]{2,0,1:T(8,128)(2,1)}), bf16[16,16,1024]{2,0,1:T(8,128)(2,1)S(1)}, u32[]{:S(2)}, u32[]{:S(2)}) %all-to-all-start.5) | async-done | bytes 524320 | tf_op jit(solution)/shard_map/all_to_all | solution.py:147
  137.3 7.5 %all-to-all-start.3 = ((bf16[32,3,4096]{2,1,0:T(4,128)(2,1)}), bf16[32,3,4096]{2,1,0:T(4,128)(2,1)S(1)}, u32[]{:S(2)}, u32[]{:S(2)}) async-start(bf16[32,3,4096]{2,1,0:T(4,128)(2,1)} %select_select_fusion), calls=%async_computation.3 | async-start | bytes 2097152 | tf_op jit(solution)/shard_map/all_to_all | solution.py:170
  144.8 14.3 %fusion.1 = bf16[32,1,16,64,256]{4,3,2,1,0:T(8,128)(2,1)} fusion(bf16[32,16,64,256]{3,2,1,0:T(8,128)(2,1)} %gather_fusion.5, pred[32]{0:T(512)(128)(4,1)S(1)} %compare_and_fusion.10, pred[32]{0:T(512)(128)(4,1)S(1)} %copy-done.19), kind=kLoop, calls=%fused_computation.9 | loop fusion | flops 16777216 | bytes 33554496 | tf_op jit(solution)/shard_map/jit(_where)/select_n | solution.py:41
  159.1 10.3 %all-to-all-done.3 = bf16[32,3,4096]{2,1,0:T(4,128)(2,1)S(1)} async-done(((bf16[32,3,4096]{2,1,0:T(4,128)(2,1)}), bf16[32,3,4096]{2,1,0:T(4,128)(2,1)S(1)}, u32[]{:S(2)}, u32[]{:S(2)}) %all-to-all-start.3) | async-done | bytes 786464 | tf_op jit(solution)/shard_map/all_to_all | solution.py:170
  169.4 0.9 copy-done.5
  170.3 6.8 %all-to-all-start.4 = ((bf16[32,1,16,64,256]{4,3,2,1,0:T(8,128)(2,1)}), bf16[32,1,16,64,256]{4,3,2,1,0:T(8,128)(2,1)}, u32[]{:S(2)}, u32[]{:S(2)}) async-start(bf16[32,1,16,64,256]{4,3,2,1,0:T(8,128)(2,1)} %fusion.1), calls=%async_computation.4 | async-start | bytes 33554432 | tf_op jit(solution)/shard_map/all_to_all | solution.py:156
  180.4 1.6 gather_fusion.2
  182.0 1.4 fusion.45
  183.4 1.4 fusion.43
  184.8 1.4 fusion.41
  187.0 1.8 multiply_convert_fusion.4
  189.3 1.7 reshape.532
  191.0 1.2 convert_bitcast_fusion
  192.1 1.9 reshape.545
  194.0 2.1 gather_fusion.4
  196.1 31.9 %all-gather.2.cloned.1.call-done = bf16[256,4096]{1,0:T(8,128)(2,1)} async-done(((bf16[16,4096]{1,0:T(8,128)(2,1)}), bf16[256,4096]{1,0:T(8,128)(2,1)}) %all-gather.2.cloned.1.call-update) | async-done | bytes 2097168 | tf_op jit(solution)/shard_map/all_gather | solution.py:150
  228.0 2.5 fusion.42
  232.1 0.9 fusion.5
  233.0 1.5 fusion.4
  234.6 1.7 multiply_convert_fusion
  236.3 1.4 copy-done.11
  238.0 301.8 %all-to-all-done.4 = bf16[32,1,16,64,256]{4,3,2,1,0:T(8,128)(2,1)} async-done(((bf16[32,1,16,64,256]{4,3,2,1,0:T(8,128)(2,1)}), bf16[32,1,16,64,256]{4,3,2,1,0:T(8,128)(2,1)}, u32[]{:S(2)}, u32[]{:S(2)}) %all-to-all-start.4) | async-done | bytes 16777248 | tf_op jit(solution)/shard_map/all_to_all | solution.py:156
  539.8 8.6 %gather_fusion.6 = bf16[8,16,64,256]{3,2,1,0:T(8,128)(2,1)} fusion(bf16[32,16,64,256]{3,2,1,0:T(8,128)(2,1)} %bitcast.31, s32[1024]{0:T(1024)} %copy-done.17), kind=kCustom, calls=%fused_computation.6 | custom fusion | bytes 8388640 | tf_op jit(solution)/shard_map/jit(_take)/gather | solution.py:178
  548.4 4.7 fusion.8
  553.2 4.7 multiply_reduce_fusion
  557.8 70.6 %psum.15 = f32[8,32,8]{1,0,2:T(8,128)S(1)} all-reduce(f32[8,32,8]{1,0,2:T(8,128)S(1)} %bitcast_dynamic-update-slice_fusion), channel_id=1, replica_groups=mesh['req'=16,'head'=16] {'head'}, use_global_device_ids=true, to_apply=%region_11.12 | all-reduce | flops 2048 | bytes 16384 | tf_op jit(solution)/shard_map/psum | solution.py:227
  628.4 1.9 multiply_convert_fusion.1
  630.8 1.5 convert_element_type.240
  (110 shorter events, 12.5 us)
Async XLA Ops:
  6.5 50.5 %copy-start = (bf16[8,32,2048]{2,1,0:T(8,128)(2,1)S(1)}, bf16[8,32,2048]{2,1,0:T(8,128)(2,1)}, u32[]{:S(2)}) copy-start(bf16[8,32,2048]{2,1,0:T(8,128)(2,1)} %param.37) | copy-start | bytes 3145732
  8.2 23.3 %all-to-all-start.2 = ((bf16[16,2,128]{2,1,0:T(2,128)(2,1)}), bf16[16,2,128]{2,1,0:T(2,128)(2,1)S(1)}, u32[]{:S(2)}, u32[]{:S(2)}) async-start(bf16[16,2,128]{2,1,0:T(2,128)(2,1)} %reshape.611), calls=%async_computation.2 | async-start | bytes 16384 | tf_op jit(solution)/shard_map/all_to_all | solution.py:148
  15.2 104.5 %all-reduce.2.cloned.1.call-start = ((), (), s32[]{:S(2)}) async-start(), calls=%async_computation.7 | async-start | bytes 524288 | tf_op jit(solution)/shard_map/psum | solution.py:113
  16.0 2.0 copy-start.20
  18.2 22.1 %copy-start.9 = (f32[8,32,16]{1,2,0:T(8,128)S(1)}, f32[8,32,16]{1,2,0:T(8,128)}, u32[]{:S(2)}) copy-start(f32[8,32,16]{1,2,0:T(8,128)} %param.38) | copy-start | bytes 49156
  20.2 20.9 %copy-start.8 = (s32[8,32,32]{2,1,0:T(8,128)S(1)}, s32[8,32,32]{2,1,0:T(8,128)}, u32[]{:S(2)}) copy-start(s32[8,32,32]{2,1,0:T(8,128)} %param.41) | copy-start | bytes 98308
  21.6 18.5 %copy-start.18 = (pred[32]{0:T(512)(128)(4,1)}, pred[32]{0:T(512)(128)(4,1)S(1)}, u32[]{:S(2)}) copy-start(pred[32]{0:T(512)(128)(4,1)S(1)} %fusion.68) | copy-start | bytes 100
  31.5 18.3 %all-to-all-start.1 = ((bf16[32,3,1024]{2,1,0:T(4,128)(2,1)}), bf16[32,3,1024]{2,1,0:T(4,128)(2,1)}, u32[]{:S(2)}, u32[]{:S(2)}) async-start(bf16[32,3,1024]{2,1,0:T(4,128)(2,1)} %select_select_fusion.1), calls=%async_computation.1 | async-start | bytes 524288 | tf_op jit(solution)/shard_map/all_to_all | solution.py:163
  49.7 72.4 %all-to-all-start = ((bf16[16,16,1024]{2,0,1:T(8,128)(2,1)}), bf16[16,16,1024]{2,0,1:T(8,128)(2,1)}, u32[]{:S(2)}, u32[]{:S(2)}) async-start(bf16[16,16,1024]{2,0,1:T(8,128)(2,1)} %bitcast.122), calls=%async_computation | async-start | bytes 1048576 | tf_op jit(solution)/shard_map/all_to_all | solution.py:146
  62.7 64.5 %copy-start.19 = (pred[32]{0:T(512)(128)(4,1)S(1)}, pred[32]{0:T(512)(128)(4,1)}, u32[]{:S(2)}) copy-start(pred[32]{0:T(512)(128)(4,1)} %copy-done.18) | copy-start | bytes 100
  122.1 15.1 %all-to-all-start.5 = ((bf16[16,16,1024]{2,0,1:T(8,128)(2,1)}), bf16[16,16,1024]{2,0,1:T(8,128)(2,1)S(1)}, u32[]{:S(2)}, u32[]{:S(2)}) async-start(bf16[16,16,1024]{2,0,1:T(8,128)(2,1)} %bitcast.116), calls=%async_computation.5 | async-start | bytes 1048576 | tf_op jit(solution)/shard_map/all_to_all | solution.py:147
  137.3 21.8 %copy-start.3 = (bf16[16,16,1024]{2,0,1:T(8,128)(2,1)}, bf16[16,16,1024]{2,0,1:T(8,128)(2,1)S(1)}, u32[]{:S(2)}) copy-start(bf16[16,16,1024]{2,0,1:T(8,128)(2,1)S(1)} %all-to-all-done.5) | copy-start | bytes 1572868
  137.3 32.1 %all-to-all-start.3 = ((bf16[32,3,4096]{2,1,0:T(4,128)(2,1)}), bf16[32,3,4096]{2,1,0:T(4,128)(2,1)S(1)}, u32[]{:S(2)}, u32[]{:S(2)}) async-start(bf16[32,3,4096]{2,1,0:T(4,128)(2,1)} %select_select_fusion), calls=%async_computation.3 | async-start | bytes 2097152 | tf_op jit(solution)/shard_map/all_to_all | solution.py:170
  159.0 19.1 %copy-start.22 = (s32[128]{0:T(128)S(1)}, s32[128]{0:T(128)}, u32[]{:S(2)}) copy-start(s32[128]{0:T(128)} %param.43) | copy-start | bytes 1540
  159.0 20.0 %copy-start.6 = (s32[8,32,32]{2,1,0:T(8,128)S(1)}, s32[8,32,32]{2,1,0:T(8,128)}, u32[]{:S(2)}) copy-start(s32[8,32,32]{2,1,0:T(8,128)} %param.26) | copy-start | bytes 98308
  159.0 20.2 %copy-start.21 = (f32[1024]{0:T(1024)S(1)}, f32[1024]{0:T(1024)}, u32[]{:S(2)}) copy-start(f32[1024]{0:T(1024)} %param.34) | copy-start | bytes 12292
  159.0 20.3 %copy-start.12 = (bf16[4,1024]{1,0:T(4,128)(2,1)S(1)}, bf16[4,1024]{1,0:T(4,128)(2,1)}, u32[]{:S(2)}) copy-start(bf16[4,1024]{1,0:T(4,128)(2,1)} %param.27) | copy-start | bytes 24580
  159.1 20.3 %copy-start.10 = (bf16[4,4096]{1,0:T(4,128)(2,1)S(1)}, bf16[4,4096]{1,0:T(4,128)(2,1)}, u32[]{:S(2)}) copy-start(bf16[4,4096]{1,0:T(4,128)(2,1)} %param.29) | copy-start | bytes 98308
  169.4 0.9 copy-start.5
  170.3 369.5 %all-to-all-start.4 = ((bf16[32,1,16,64,256]{4,3,2,1,0:T(8,128)(2,1)}), bf16[32,1,16,64,256]{4,3,2,1,0:T(8,128)(2,1)}, u32[]{:S(2)}, u32[]{:S(2)}) async-start(bf16[32,1,16,64,256]{4,3,2,1,0:T(8,128)(2,1)} %fusion.1), calls=%async_computation.4 | async-start | bytes 33554432 | tf_op jit(solution)/shard_map/all_to_all | solution.py:156
  177.2 50.9 %all-gather.2.cloned.1.call-start = ((), (), s32[]{:S(2)}) async-start(), calls=%async_computation.6 | async-start | bytes 2228224 | tf_op jit(solution)/shard_map/all_gather | solution.py:150
  179.0 8.0 %copy-start.15 = (pred[8]{0:T(512)(128)(4,1)}, pred[8]{0:T(512)(128)(4,1)S(1)}, u32[]{:S(2)}) copy-start(pred[8]{0:T(512)(128)(4,1)S(1)} %compare_and_fusion.11) | copy-start | bytes 28
  179.3 7.6 %copy-start.17 = (s32[1024]{0:T(1024)}, s32[1024]{0:T(1024)S(1)}, u32[]{:S(2)}) copy-start(s32[1024]{0:T(1024)S(1)} %pad_clamp_fusion) | copy-start | bytes 12292
  183.3 3.6 copy-start.23
  228.0 2.5 copy-start.2
  231.3 0.8 copy-start.16
  232.1 0.9 copy-start.14
  233.0 1.6 copy-start.13
  236.3 1.4 copy-start.11
  548.4 4.7 copy-start.4
  548.4 4.7 copy-start.7
  548.4 4.7 copy-start.24
  553.2 79.1 %copy-start.1 = (bf16[8,32,2048]{2,1,0:T(8,128)(2,1)S(1)}, bf16[8,32,2048]{2,1,0:T(8,128)(2,1)}, u32[]{:S(2)}) copy-start(bf16[8,32,2048]{2,1,0:T(8,128)(2,1)} %param.37) | copy-start | bytes 3145732
Sparse Core Ops, SparseCore 0:
  20.4 99.3 all-reduce.1
  180.4 47.5 all-gather.1
where the time goes:
time: 641 us; the launch traced here: 639 us
  waiting for transfers between devices  408 us (64%)
  blocking collectives  70.6 us (11%)
  local copies, waits for them, and re-layouts  42.5 us (7%)
  starting transfers between devices  42.5 us (7%)
  matrix products  34.7 us (5%)
  other arithmetic  26.6 us (4%)
  between operations  14.1 us (2%)
    all_to_all x1, waiting for transfers between devices, shards(): lax.all_to_all(place_slots(carry_state, send_pos, slot_count), 'req', spl...  302 us
    psum x1, blocking collectives, shards(): power_total = lax.psum(power_full, 'head')  70.6 us
    psum x1, waiting for transfers between devices, shards(): tail_groups = lax.psum(tail_part.astype(jnp.bfloat16), 'head')  47.8 us
    all_gather x1, waiting for transfers between devices, shards(): group_rows = lax.all_gather(tree_groups, 'head', axis=0, tiled=True)  31.9 us
    select_n x3, other arithmetic, place_slots(): return jnp.where(filled, taken, jnp.zeros_like(taken))  16.9 us
  transfers between devices with their start and end apart: 8, of which 6 were waited for; matrix products, arithmetic and copies ran while one was open for 12% of the time, Pallas kernels for 0%

commit v1 on v0

--- a/solution.py
+++ b/solution.py
@@ -147,7 +147,8 @@
         lax.all_to_all(tree_gates, "head", split_axis=1, concat_axis=0, tiled=True),
         lax.all_to_all(tree_steps, "head", split_axis=1, concat_axis=0, tiled=True),
     )
-    group_rows = lax.all_gather(tree_groups, "head", axis=0, tiled=True)
+    sent = jnp.stack([tree_groups] * lax.axis_size("head"))
+    group_rows = jnp.concatenate(lax.all_to_all(sent, "head", 0, 0), axis=0)
     head_rows = head_rows.reshape(reqs_dev, NODES, -1)
     gate_rows = gate_rows.reshape(reqs_dev, NODES, span_groups, span_heads, HEAD_DIM)
     step_rows = step_rows.reshape(reqs_dev, NODES, local_heads)

time: 641 us -> 704 us (1.098)
  waiting for transfers between devices: 408 us -> 469 us
    psum x1, waiting for transfers between devices: 47.8 us -> 96 us  [shards(): tail_groups = lax.psum(tail_part.astype(jnp.bfloat16), 'head')]
    all_to_all x1, waiting for transfers between devices: 302 us -> 337 us  [shards(): lax.all_to_all(place_slots(carry_state, send_pos, slot_count), 'req', spl...]
    all_gather x1 -> x0, waiting for transfers between devices: 31.9 us -> none  [shards(): group_rows = lax.all_gather(tree_groups, 'head', axis=0, tiled=True)]
    all_to_all x1, waiting for transfers between devices: 10.3 us -> 19.1 us  [shards(): lax.all_to_all(place_slots(tail_groups, send_pos, slot_count), 'req', spl...]
  transfers between devices with their start and end apart: 8 -> 8, of which waited for: 6 -> 6; matrix products, arithmetic and copies ran while one was open for 12% -> 11% of each run, Pallas kernels for 0% -> 0%
where the time goes in v1:
time: 704 us; the launch traced here: 703 us
  waiting for transfers between devices  469 us (67%)
  blocking collectives  74.6 us (11%)
  local copies, waits for them, and re-layouts  46.7 us (7%)
  starting transfers between devices  46.1 us (7%)
  matrix products  28.1 us (4%)
  other arithmetic  24.3 us (3%)
  between operations  14.1 us (2%)
    all_to_all x1, waiting for transfers between devices, shards(): lax.all_to_all(place_slots(carry_state, send_pos, slot_count), 'req', spl...  337 us
    psum x1, waiting for transfers between devices, shards(): tail_groups = lax.psum(tail_part.astype(jnp.bfloat16), 'head')  96 us
    psum x1, blocking collectives, shards(): power_total = lax.psum(power_full, 'head')  74.6 us
    all_to_all x1, waiting for transfers between devices, shards(): lax.all_to_all(place_slots(tail_groups, send_pos, slot_count), 'req', spl...  19.1 us
    select_n x3, other arithmetic, place_slots(): return jnp.where(filled, taken, jnp.zeros_like(taken))  16.9 us
  transfers between devices with their start and end apart: 8, of which 6 were waited for; matrix products, arithmetic and copies ran while one was open for 11% of the time, Pallas kernels for 0%

profile of v1, /device:TPU:32, one launch (start us, length us, event | category | flops | bytes accessed | tf_op | source)
XLA Modules:
  0.0 702.7 jit_solution(17079442492796601729)
XLA Ops:
  6.5 0.9 copy.90
  8.2 7.0 %all-to-all-start.2 = ((bf16[16,2,128]{2,1,0:T(2,128)(2,1)}), bf16[16,2,128]{2,1,0:T(2,128)(2,1)S(1)}, u32[]{:S(2)}, u32[]{:S(2)}) async-start(bf16[16,2,128]{2,1,0:T(2,128)(2,1)} %reshape.609), calls=%async_computation.2 | async-start | bytes 16384 | tf_op jit(solution)/shard_map/all_to_all | solution.py:148
  17.3 1.2 fusion.81
  18.5 0.8 broadcast_add_fusion.4
  19.4 1.4 convolution_convert_fusion.1
  20.9 0.8 gather_fusion.1
  21.6 1.0 select_select_fusion.1
  22.8 8.6 %all-to-all-start.1 = ((bf16[32,3,1024]{2,1,0:T(4,128)(2,1)}), bf16[32,3,1024]{2,1,0:T(4,128)(2,1)S(1)}, u32[]{:S(2)}, u32[]{:S(2)}) async-start(bf16[32,3,1024]{2,1,0:T(4,128)(2,1)} %select_select_fusion.1), calls=%async_computation.1 | async-start | bytes 524288 | tf_op jit(solution)/shard_map/all_to_all | solution.py:164
  31.4 1.9 copy.134
  33.3 7.7 %all-to-all-done.1 = bf16[32,3,1024]{2,1,0:T(4,128)(2,1)S(1)} async-done(((bf16[32,3,1024]{2,1,0:T(4,128)(2,1)}), bf16[32,3,1024]{2,1,0:T(4,128)(2,1)S(1)}, u32[]{:S(2)}, u32[]{:S(2)}) %all-to-all-start.1) | async-done | bytes 196640 | tf_op jit(solution)/shard_map/all_to_all | solution.py:164
  41.7 7.0 all-to-all-start
  48.9 1.1 convolution_convert_fusion
  50.0 0.8 copy.133
  50.9 96.0 %all-reduce.2.cloned.1.call-done = bf16[8,3,4096]{2,1,0:T(4,128)(2,1)} async-done(((bf16[8,3,4096]{2,1,0:T(4,128)(2,1)}), bf16[8,3,4096]{2,1,0:T(4,128)(2,1)}) %all-reduce.2.cloned.1.call-update) | async-done | bytes 196624 | tf_op jit(solution)/shard_map/psum | solution.py:113
  146.9 2.4 gather_fusion.3
  149.3 5.2 all-to-all-start.6
  154.5 1.7 select_select_fusion
  156.3 8.3 %all-to-all-done.6 = bf16[16,16,1024]{2,0,1:T(8,128)(2,1)S(1)} async-done(((bf16[16,16,1024]{2,0,1:T(8,128)(2,1)}), bf16[16,16,1024]{2,0,1:T(8,128)(2,1)S(1)}, u32[]{:S(2)}, u32[]{:S(2)}) %all-to-all-start.6) | async-done | bytes 524320 | tf_op jit(solution)/shard_map/all_to_all | solution.py:147
  164.6 7.5 %all-to-all-start.4 = ((bf16[32,3,4096]{2,1,0:T(4,128)(2,1)}), bf16[32,3,4096]{2,1,0:T(4,128)(2,1)S(1)}, u32[]{:S(2)}, u32[]{:S(2)}) async-start(bf16[32,3,4096]{2,1,0:T(4,128)(2,1)} %select_select_fusion), calls=%async_computation.4 | async-start | bytes 2097152 | tf_op jit(solution)/shard_map/all_to_all | solution.py:171
  172.1 2.8 reshape.541
  175.7 0.8 broadcast_multiply_fusion
  176.5 1.1 select_reduce_fusion.1
  177.7 19.1 %all-to-all-done.4 = bf16[32,3,4096]{2,1,0:T(4,128)(2,1)S(1)} async-done(((bf16[32,3,4096]{2,1,0:T(4,128)(2,1)}), bf16[32,3,4096]{2,1,0:T(4,128)(2,1)S(1)}, u32[]{:S(2)}, u32[]{:S(2)}) %all-to-all-start.4) | async-done | bytes 786464 | tf_op jit(solution)/shard_map/all_to_all | solution.py:171
  196.7 2.6 stack.2
  199.3 3.7 all-to-all-start.3
  203.1 7.1 %add_convert_fusion = bf16[8,16,64,256]{3,2,1,0:T(8,128)(2,1)} fusion(bf16[8,16,64,256]{3,2,1,0:T(8,128)(2,1)} %param.35, f32[8,16]{1,0:T(8,128)S(1)} %exp.56, f32[8,32,16,64]{3,2,1,0:T(8,128)} %reshape.541, f32[8,32,16]{1,2,0:T(8,128)S(1)} %bitcast_multiply_fusion.1, bf16[8,32,2048]{2,1,0:T(8,128)(2,1)S(1)} %copy-done, s32[]{:T(128)S(6)} %select_n.269), kind=kOutput, calls=%fused_computation.10 | convolution fusion | flops 143130624 | bytes 9637892 | tf_op jit(solution)/shard_map/bjgqp,bjgn->bgqpn/dot_general | solution.py:137
  210.2 9.3 %gather_fusion.5 = bf16[32,16,64,256]{3,2,1,0:T(8,128)(2,1)} fusion(bf16[8,16,64,256]{3,2,1,0:T(8,128)(2,1)} %add_convert_fusion, s32[1024]{0:T(1024)S(1)} %pad_clamp_fusion.1), kind=kCustom, calls=%fused_computation.5 | custom fusion | bytes 33554560 | tf_op jit(solution)/shard_map/jit(_take)/gather | solution.py:40
  219.5 14.3 %fusion.1 = bf16[32,1,16,64,256]{4,3,2,1,0:T(8,128)(2,1)} fusion(bf16[32,16,64,256]{3,2,1,0:T(8,128)(2,1)} %gather_fusion.5, pred[32]{0:T(512)(128)(4,1)S(1)} %compare_and_fusion.10, pred[32]{0:T(512)(128)(4,1)S(1)} %copy-done.22), kind=kLoop, calls=%fused_computation.9 | loop fusion | flops 16777216 | bytes 33554496 | tf_op jit(solution)/shard_map/jit(_where)/select_n | solution.py:41
  233.8 7.1 %all-to-all-start.5 = ((bf16[32,1,16,64,256]{4,3,2,1,0:T(8,128)(2,1)}), bf16[32,1,16,64,256]{4,3,2,1,0:T(8,128)(2,1)}, u32[]{:S(2)}, u32[]{:S(2)}) async-start(bf16[32,1,16,64,256]{4,3,2,1,0:T(8,128)(2,1)} %fusion.1), calls=%async_computation.5 | async-start | bytes 33554432 | tf_op jit(solution)/shard_map/all_to_all | solution.py:157
  243.3 1.6 gather_fusion.2
  246.8 1.5 multiply_convert_fusion.4
  248.4 2.7 reshape.542
  251.1 2.5 reshape.531
  253.6 1.2 convert_bitcast_fusion
  254.7 1.9 reshape.543
  256.7 2.1 gather_fusion.4
  258.8 0.8 fusion.42
  259.6 0.7 fusion.40
  260.3 0.7 fusion.44
  261.1 0.9 fusion.5
  262.0 1.5 fusion.4
  263.6 1.7 multiply_convert_fusion
  265.6 337.5 %all-to-all-done.5 = bf16[32,1,16,64,256]{4,3,2,1,0:T(8,128)(2,1)} async-done(((bf16[32,1,16,64,256]{4,3,2,1,0:T(8,128)(2,1)}), bf16[32,1,16,64,256]{4,3,2,1,0:T(8,128)(2,1)}, u32[]{:S(2)}, u32[]{:S(2)}) %all-to-all-start.5) | async-done | bytes 16777248 | tf_op jit(solution)/shard_map/all_to_all | solution.py:157
  603.0 8.7 %gather_fusion.6 = bf16[8,16,64,256]{3,2,1,0:T(8,128)(2,1)} fusion(bf16[32,16,64,256]{3,2,1,0:T(8,128)(2,1)} %bitcast.31, s32[1024]{0:T(1024)} %copy-done.20), kind=kCustom, calls=%fused_computation.6 | custom fusion | bytes 8388640 | tf_op jit(solution)/shard_map/jit(_take)/gather | solution.py:179
  611.7 4.5 fusion.8
  616.3 2.7 multiply_reduce_fusion
  619.0 74.6 %psum.15 = f32[8,32,8]{1,0,2:T(8,128)S(1)} all-reduce(f32[8,32,8]{1,0,2:T(8,128)S(1)} %bitcast_dynamic-update-slice_fusion), channel_id=1, replica_groups=mesh['req'=16,'head'=16] {'head'}, use_global_device_ids=true, to_apply=%region_11.12 | all-reduce | flops 2048 | bytes 16384 | tf_op jit(solution)/shard_map/psum | solution.py:228
  694.4 1.5 convert_element_type.240
  (120 shorter events, 10.2 us)
Async XLA Ops:
  6.5 196.5 %copy-start = (bf16[8,32,2048]{2,1,0:T(8,128)(2,1)S(1)}, bf16[8,32,2048]{2,1,0:T(8,128)(2,1)}, u32[]{:S(2)}) copy-start(bf16[8,32,2048]{2,1,0:T(8,128)(2,1)} %param.37) | copy-start | bytes 3145732
  6.5 42.4 %copy-start.26 = (bf16[8,2,4096]{2,1,0:T(2,128)(2,1)S(1)}, bf16[8,2,4096]{2,1,0:T(2,128)(2,1)}, u32[]{:S(2)}) copy-start(bf16[8,2,4096]{2,1,0:T(2,128)(2,1)} %param.40) | copy-start | bytes 393220
  6.5 43.5 %copy-start.10 = (bf16[16,16384]{1,0:T(8,128)(2,1)S(1)}, bf16[16,16384]{1,0:T(8,128)(2,1)}, u32[]{:S(2)}) copy-start(bf16[16,16384]{1,0:T(8,128)(2,1)} %param.23) | copy-start | bytes 1572868
  8.2 14.6 %all-to-all-start.2 = ((bf16[16,2,128]{2,1,0:T(2,128)(2,1)}), bf16[16,2,128]{2,1,0:T(2,128)(2,1)S(1)}, u32[]{:S(2)}, u32[]{:S(2)}) async-start(bf16[16,2,128]{2,1,0:T(2,128)(2,1)} %reshape.609), calls=%async_computation.2 | async-start | bytes 16384 | tf_op jit(solution)/shard_map/all_to_all | solution.py:148
  16.6 137.9 %copy-start.21 = (pred[32]{0:T(512)(128)(4,1)}, pred[32]{0:T(512)(128)(4,1)S(1)}, u32[]{:S(2)}) copy-start(pred[32]{0:T(512)(128)(4,1)S(1)} %fusion.68) | copy-start | bytes 100
  17.3 1.2 copy-start.23
  22.8 18.2 %all-to-all-start.1 = ((bf16[32,3,1024]{2,1,0:T(4,128)(2,1)}), bf16[32,3,1024]{2,1,0:T(4,128)(2,1)S(1)}, u32[]{:S(2)}, u32[]{:S(2)}) async-start(bf16[32,3,1024]{2,1,0:T(4,128)(2,1)} %select_select_fusion.1), calls=%async_computation.1 | async-start | bytes 524288 | tf_op jit(solution)/shard_map/all_to_all | solution.py:164
  41.0 0.7 copy-start.12
  41.7 107.6 %all-to-all-start = ((bf16[16,16,1024]{2,0,1:T(8,128)(2,1)}), bf16[16,16,1024]{2,0,1:T(8,128)(2,1)S(1)}, u32[]{:S(2)}, u32[]{:S(2)}) async-start(bf16[16,16,1024]{2,0,1:T(8,128)(2,1)} %bitcast.117), calls=%async_computation | async-start | bytes 1048576 | tf_op jit(solution)/shard_map/all_to_all | solution.py:146
  48.7 98.2 %all-reduce.2.cloned.1.call-start = ((), (), s32[]{:S(2)}) async-start(), calls=%async_computation.7 | async-start | bytes 524288 | tf_op jit(solution)/shard_map/psum | solution.py:113
  149.3 25.6 %copy-start.28 = (f32[16]{0:T(128)S(1)}, f32[16]{0:T(128)}, u32[]{:S(2)}) copy-start(f32[16]{0:T(128)} %param.31) | copy-start | bytes 196
  149.3 26.3 %copy-start.2 = (bf16[16,16,1024]{2,0,1:T(8,128)(2,1)}, bf16[16,16,1024]{2,0,1:T(8,128)(2,1)S(1)}, u32[]{:S(2)}) copy-start(bf16[16,16,1024]{2,0,1:T(8,128)(2,1)S(1)} %all-to-all-done) | copy-start | bytes 1572868
  149.3 26.3 %copy-start.13 = (f32[8,32,16]{1,2,0:T(8,128)S(1)}, f32[8,32,16]{1,2,0:T(8,128)}, u32[]{:S(2)}) copy-start(f32[8,32,16]{1,2,0:T(8,128)} %param.38) | copy-start | bytes 49156
  149.3 15.3 %all-to-all-start.6 = ((bf16[16,16,1024]{2,0,1:T(8,128)(2,1)}), bf16[16,16,1024]{2,0,1:T(8,128)(2,1)S(1)}, u32[]{:S(2)}, u32[]{:S(2)}) async-start(bf16[16,16,1024]{2,0,1:T(8,128)(2,1)} %bitcast.126), calls=%async_computation.6 | async-start | bytes 1048576 | tf_op jit(solution)/shard_map/all_to_all | solution.py:147
  154.5 21.9 %copy-start.11 = (s32[8,32,32]{2,1,0:T(8,128)S(1)}, s32[8,32,32]{2,1,0:T(8,128)}, u32[]{:S(2)}) copy-start(s32[8,32,32]{2,1,0:T(8,128)} %param.41) | copy-start | bytes 98308
  164.6 34.7 %copy-start.5 = (bf16[16,16,1024]{2,0,1:T(8,128)(2,1)}, bf16[16,16,1024]{2,0,1:T(8,128)(2,1)S(1)}, u32[]{:S(2)}) copy-start(bf16[16,16,1024]{2,0,1:T(8,128)(2,1)S(1)} %all-to-all-done.6) | copy-start | bytes 1572868
  164.6 32.1 %all-to-all-start.4 = ((bf16[32,3,4096]{2,1,0:T(4,128)(2,1)}), bf16[32,3,4096]{2,1,0:T(4,128)(2,1)S(1)}, u32[]{:S(2)}, u32[]{:S(2)}) async-start(bf16[32,3,4096]{2,1,0:T(4,128)(2,1)} %select_select_fusion), calls=%async_computation.4 | async-start | bytes 2097152 | tf_op jit(solution)/shard_map/all_to_all | solution.py:171
  196.7 2.6 copy-start.7
  199.3 34.5 %all-to-all-start.3 = ((bf16[16,16,4096]{2,1,0:T(8,128)(2,1)}), bf16[16,16,4096]{2,1,0:T(8,128)(2,1)S(1)}, u32[]{:S(2)}, u32[]{:S(2)}) async-start(bf16[16,16,4096]{2,1,0:T(8,128)(2,1)} %stack.2), calls=%async_computation.3 | async-start | bytes 4194304 | tf_op jit(solution)/shard_map/all_to_all | solution.py:151
  210.2 9.3 %copy-start.22 = (pred[32]{0:T(512)(128)(4,1)S(1)}, pred[32]{0:T(512)(128)(4,1)}, u32[]{:S(2)}) copy-start(pred[32]{0:T(512)(128)(4,1)} %copy-done.21) | copy-start | bytes 100
  233.8 7.3 %copy-start.8 = (s32[8,32,32]{2,1,0:T(8,128)S(1)}, s32[8,32,32]{2,1,0:T(8,128)}, u32[]{:S(2)}) copy-start(s32[8,32,32]{2,1,0:T(8,128)} %param.26) | copy-start | bytes 98308
  233.8 7.5 %copy-start.24 = (f32[1024]{0:T(1024)S(1)}, f32[1024]{0:T(1024)}, u32[]{:S(2)}) copy-start(f32[1024]{0:T(1024)} %param.34) | copy-start | bytes 12292
  233.8 7.6 %copy-start.25 = (s32[128]{0:T(128)S(1)}, s32[128]{0:T(128)}, u32[]{:S(2)}) copy-start(s32[128]{0:T(128)} %param.43) | copy-start | bytes 1540
  233.8 8.5 %copy-start.15 = (bf16[4,1024]{1,0:T(4,128)(2,1)S(1)}, bf16[4,1024]{1,0:T(4,128)(2,1)}, u32[]{:S(2)}) copy-start(bf16[4,1024]{1,0:T(4,128)(2,1)} %param.27) | copy-start | bytes 24580
  233.8 8.6 %copy-start.14 = (bf16[4,4096]{1,0:T(4,128)(2,1)S(1)}, bf16[4,4096]{1,0:T(4,128)(2,1)}, u32[]{:S(2)}) copy-start(bf16[4,4096]{1,0:T(4,128)(2,1)} %param.29) | copy-start | bytes 98308
  233.8 11.1 %copy-start.3 = (bf16[16,16,1024]{2,0,1:T(8,128)(2,1)S(1)}, bf16[16,16,1024]{2,0,1:T(8,128)(2,1)}, u32[]{:S(2)}) copy-start(bf16[16,16,1024]{2,0,1:T(8,128)(2,1)} %copy-done.2) | copy-start | bytes 1572868
  233.8 369.2 %all-to-all-start.5 = ((bf16[32,1,16,64,256]{4,3,2,1,0:T(8,128)(2,1)}), bf16[32,1,16,64,256]{4,3,2,1,0:T(8,128)(2,1)}, u32[]{:S(2)}, u32[]{:S(2)}) async-start(bf16[32,1,16,64,256]{4,3,2,1,0:T(8,128)(2,1)} %fusion.1), calls=%async_computation.5 | async-start | bytes 33554432 | tf_op jit(solution)/shard_map/all_to_all | solution.py:157
  242.2 4.6 copy-start.20
  242.3 4.5 copy-start.18
  245.3 1.5 copy-start.27
  260.3 0.8 copy-start.19
  261.1 0.9 copy-start.17
  262.0 1.6 copy-start.16
  611.7 4.5 copy-start.4
  611.7 4.5 copy-start.6
  611.7 4.5 copy-start.9
  611.7 4.5 copy-start.29
  616.2 79.6 %copy-start.1 = (bf16[8,32,2048]{2,1,0:T(8,128)(2,1)S(1)}, bf16[8,32,2048]{2,1,0:T(8,128)(2,1)}, u32[]{:S(2)}) copy-start(bf16[8,32,2048]{2,1,0:T(8,128)(2,1)} %param.37) | copy-start | bytes 3145732
Sparse Core Ops, SparseCore 0:
  52.7 94.1 all-reduce.1
